TPU v7x, 32 devices: a whole 2x2x4 slice. The times are simulated.
32 devices in a mesh: seq: 16 (over z, y, x), grp: 2 (over core).
Axes of the slice: x: 2, y: 2, z: 4, core: 2. Of those that a mesh axis runs over, the one named last changes fastest.
Arguments:
- queries: bfloat16 [4096, 2048], P('seq', 'grp'), parts along dimension 1, may hold values from -80 to 80
- shared_keys: bfloat16 [4096, 256], P('seq', 'grp'), parts along dimension 1, may hold values from -4 to 4
- shared_values: bfloat16 [4096, 256], P('seq', 'grp'), parts along dimension 1, may hold values from -6 to 6
- outputs: bfloat16 [4096, 2048], P('seq', 'grp'), parts along dimension 1, may hold values from -6 to 6
- out_grad: bfloat16 [4096, 2048], P('seq', 'grp'), parts along dimension 1, may hold values from -6 to 6
- doc_lengths: int32 [64], replicated, may hold values from 1 to 2048, 4096 in all
Outputs:
- grad_queries: bfloat16 [4096, 2048], P('seq', 'grp'), parts along dimension 1
- grad_keys: bfloat16 [4096, 256], P('seq', 'grp'), parts along dimension 1
- grad_values: bfloat16 [4096, 256], P('seq', 'grp'), parts along dimension 1
There are 2 independent parts, one for each index of `grp`. A program takes and returns all parts, laid end to end along the dimension named above; an argument that names none is the same for every part. Nothing has to cross between parts.
Inputs may be any that keep to these rules, and one draw needn't show every extreme that they name: `doc_lengths`: lengths of the 64 documents in packing order; they sum to 4096 and the longest is exactly 2048.
All inputs are finite; a program needn't handle non-finite values.
Results may differ from a plain program's by a relative error of at most 0.0051.
Values may be sent and summed in bfloat16 or wider, within the bound.
No kernel may reach another device: no remote copies, remote signals or barrier semaphores. Data moves between devices by JAX's collectives and lax.ppermute only.
A program may use at most 64 MiB of HBM per device.

v0:
```python
import functools

import jax
import jax.numpy as jnp
from jax import lax
from jax.experimental import pallas as pl
from jax.experimental.pallas import tpu as pltpu
from jax.sharding import PartitionSpec as P

REACH = 16


def _bwd_kernel(blk_ref, kb0_ref, q_ref, do_ref, kv_ref, kt_ref, begin_ref, qpos_ref,
                delta_ref, dq_ref, dkv_ref, qall, doall, dqt,
                *, rows, heads, width, reach, scaling):
    s = pl.program_id(0)
    b = blk_ref[s]
    kb0 = kb0_ref[s]
    for h in range(heads):
        qall[h * rows:(h + 1) * rows, :] = q_ref[:, h * width:(h + 1) * width]
        doall[h * rows:(h + 1) * rows, :] = do_ref[:, h * width:(h + 1) * width]
    begin = begin_ref[...]
    qpos = qpos_ref[...]
    delta = delta_ref[...]
    dqt[...] = jnp.zeros(dqt.shape, jnp.float32)
    dkv_ref[...] = jnp.zeros(dkv_ref.shape, jnp.float32)
    k_iota = lax.broadcasted_iota(jnp.int32, (rows, 1), 0)
    base = (b - reach) * rows
    nt = (((1,), (1,)), ((), ()))

    def scores(c):
        kc = kv_ref[c, :, :width]
        st = lax.dot_general(kc, qall[...], nt, preferred_element_type=jnp.float32) * scaling
        kpos = base + c * rows + k_iota
        allowed = (kpos >= begin) & (kpos <= qpos)
        return st, allowed

    def stat_step(c, carry):
        m, l = carry
        st, allowed = scores(c)
        masked = jnp.where(allowed, st, -1e30)
        m_new = jnp.maximum(m, jnp.max(masked, axis=0, keepdims=True))
        e = jnp.where(allowed, jnp.exp(st - m_new), 0.0)
        l = l * jnp.exp(m - m_new) + jnp.sum(e, axis=0, keepdims=True)
        return m_new, l

    cols = heads * rows
    m0 = jnp.full((1, cols), -1e30, jnp.float32)
    l0 = jnp.zeros((1, cols), jnp.float32)
    m, l = lax.fori_loop(kb0, reach + 1, stat_step, (m0, l0))
    lse = m + jnp.log(l)

    def grad_step(c, carry):
        st, allowed = scores(c)
        p = jnp.where(allowed, jnp.exp(st - lse), 0.0)
        vc = kv_ref[c, :, width:]
        dpt = lax.dot_general(vc, doall[...], nt, preferred_element_type=jnp.float32)
        ds = (p * (dpt - delta)).astype(jnp.bfloat16)
        pb = p.astype(jnp.bfloat16)
        dk = jnp.dot(ds, qall[...], preferred_element_type=jnp.float32) * scaling
        dv = jnp.dot(pb, doall[...], preferred_element_type=jnp.float32)
        dkv_ref[c, :, :width] = dk
        dkv_ref[c, :, width:] = dv
        dqt[...] += jnp.dot(kt_ref[c], ds, preferred_element_type=jnp.float32)
        return carry

    lax.fori_loop(kb0, reach + 1, grad_step, 0)
    for h in range(heads):
        piece = dqt[:, h * rows:(h + 1) * rows]
        dq_ref[:, h * width:(h + 1) * width] = (piece.T * scaling).astype(jnp.bfloat16)


def body(queries, shared_keys, shared_values, outputs, out_grad, doc_lengths):
    n_in = lax.axis_size("w")
    rank = lax.axis_index("zp") * n_in + lax.axis_index("w")
    n_out = lax.axis_size("zp")
    n_seq = n_out * n_in
    rows = shared_keys.shape[0] // 2
    width = shared_keys.shape[1]
    heads = queries.shape[1] // width
    scaling = width ** (-0.5)
    win = REACH + 1
    doc_ends = jnp.cumsum(doc_lengths)
    doc_starts = doc_ends - doc_lengths
    blocks = jnp.stack([rank, 2 * n_seq - 1 - rank]).astype(jnp.int32)

    kv_local = jnp.concatenate([shared_keys, shared_values], axis=1)
    kv_col = lax.all_to_all(
        jnp.broadcast_to(kv_local[None], (n_out,) + kv_local.shape), "zp", 0, 0
    )
    kv_all = lax.all_to_all(
        jnp.broadcast_to(kv_col[None], (n_in,) + kv_col.shape), "w", 0, 0
    )
    kv_st = jnp.swapaxes(kv_all, 0, 1).reshape(n_seq, 2, rows, 2 * width)
    kv_seq = jnp.concatenate(
        [jnp.zeros((REACH, rows, 2 * width), kv_all.dtype), kv_st[:, 0], kv_st[::-1, 1]], axis=0
    )
    windows = jnp.stack(
        [lax.dynamic_slice_in_dim(kv_seq, blocks[i], win, 0) for i in range(2)]
    )
    kt = jnp.swapaxes(windows[..., :width], 2, 3)

    base_pos = jnp.arange(rows, dtype=jnp.int32)
    pos = blocks[:, None] * rows + base_pos[None, :]
    begins = jnp.max(
        jnp.where(doc_starts[None, None, :] <= pos[:, :, None], doc_starts[None, None, :], 0), axis=2
    ).astype(jnp.int32)
    kb0 = jnp.maximum(0, begins[:, 0] // rows - (blocks - REACH)).astype(jnp.int32)
    begin_t = jnp.tile(begins, (1, heads)).reshape(2, 1, heads * rows)
    qpos_t = jnp.tile(pos, (1, heads)).reshape(2, 1, heads * rows)
    prod = out_grad.astype(jnp.float32) * outputs.astype(jnp.float32)
    deltas = jnp.sum(prod.reshape(2, rows, heads, width), axis=3)
    delta_t = jnp.swapaxes(deltas, 1, 2).reshape(2, 1, heads * rows)

    kernel = functools.partial(
        _bwd_kernel, rows=rows, heads=heads, width=width, reach=REACH, scaling=scaling
    )
    cols = heads * rows
    grid_spec = pltpu.PrefetchScalarGridSpec(
        num_scalar_prefetch=2,
        grid=(2,),
        in_specs=[
            pl.BlockSpec((rows, cols), lambda s, blk, k0: (s, 0)),
            pl.BlockSpec((rows, cols), lambda s, blk, k0: (s, 0)),
            pl.BlockSpec((None, win, rows, 2 * width), lambda s, blk, k0: (s, 0, 0, 0)),
            pl.BlockSpec((None, win, width, rows), lambda s, blk, k0: (s, 0, 0, 0)),
            pl.BlockSpec((None, 1, cols), lambda s, blk, k0: (s, 0, 0)),
            pl.BlockSpec((None, 1, cols), lambda s, blk, k0: (s, 0, 0)),
            pl.BlockSpec((None, 1, cols), lambda s, blk, k0: (s, 0, 0)),
        ],
        out_specs=[
            pl.BlockSpec((rows, cols), lambda s, blk, k0: (s, 0)),
            pl.BlockSpec((None, win, rows, 2 * width), lambda s, blk, k0: (s, 0, 0, 0)),
        ],
        scratch_shapes=[
            pltpu.VMEM((cols, width), jnp.bfloat16),
            pltpu.VMEM((cols, width), jnp.bfloat16),
            pltpu.VMEM((width, cols), jnp.float32),
        ],
    )
    flops = 2 * 2 * win * 6 * rows * cols * width
    grad_queries, partial = pl.pallas_call(
        kernel,
        grid_spec=grid_spec,
        out_shape=[
            jax.ShapeDtypeStruct((2 * rows, cols), jnp.bfloat16),
            jax.ShapeDtypeStruct((2, win, rows, 2 * width), jnp.float32),
        ],
        compiler_params=pltpu.CompilerParams(dimension_semantics=("arbitrary",)),
        cost_estimate=pl.CostEstimate(
            flops=flops, transcendentals=2 * 2 * win * rows * cols, bytes_accessed=8 << 20
        ),
    )(blocks, kb0, queries, out_grad, windows, kt, begin_t, qpos_t, delta_t)

    acc = jnp.zeros((2 * n_seq + REACH, rows, 2 * width), jnp.float32)
    acc = lax.dynamic_update_slice_in_dim(acc, partial[0], blocks[0], 0)
    cur = lax.dynamic_slice_in_dim(acc, blocks[1], win, 0)
    acc = lax.dynamic_update_slice_in_dim(acc, cur + partial[1], blocks[1], 0)
    acc = acc[REACH:]
    storage = jnp.stack([acc[:n_seq], acc[n_seq:][::-1]], axis=1)
    storage = storage.reshape(n_out, n_in, 2, rows, 2 * width).astype(jnp.bfloat16)
    plane = lax.all_to_all(storage, "w", 1, 1)
    plane = jnp.sum(plane.astype(jnp.float32), axis=1)
    column = lax.all_to_all(plane, "zp", 0, 0)
    summed = jnp.sum(column, axis=0).reshape(2 * rows, 2 * width)
    grad_keys = summed[:, :width].astype(jnp.bfloat16)
    grad_values = summed[:, width:].astype(jnp.bfloat16)
    return (grad_queries, grad_keys, grad_values)


GROUP = 4


def solution(mesh):
    n_seq, n_grp = mesh.devices.shape
    split = mesh.devices.reshape(n_seq // GROUP, GROUP, n_grp)
    mesh2 = jax.sharding.Mesh(split, ("zp", "w", "grp"))
    rows = P(("zp", "w"), "grp")
    placed = (rows, rows, rows, rows, rows, P())
    return jax.shard_map(
        body,
        mesh=mesh2,
        in_specs=placed,
        out_specs=(rows, rows, rows),
        check_vma=False,
    )
```

profile of v0, /device:TPU:0, one launch (start us, length us, event | category | flops | bytes accessed | tf_op | source)
XLA Modules:
  0.0 148.0 jit_solution(9075746022976331041)
XLA Ops:
  0.6 0.9 pad_maximum_fusion.3
  1.6 20.6 %all_to_all.20 = bf16[4,256,256]{2,1,0:T(8,128)(2,1)S(1)} all-to-all(bf16[4,256,256]{2,1,0:T(8,128)(2,1)S(1)} %broadcast_in_dim.16), channel_id=1, replica_groups=mesh['zp'=4,'w'=4,'grp'=2] {'zp'}, dimensions={0} | all-to-all | bytes 1048576 | tf_op jit(solution)/shard_map/all_to_all | solution.py:88
  22.2 1.6 %broadcast_in_dim.17 = bf16[4,4,256,256]{3,2,1,0:T(8,128)(2,1)} broadcast(bf16[4,256,256]{2,1,0:T(8,128)(2,1)S(1)} %all_to_all.20), dimensions={1,2,3} | broadcast | bytes 2621440 | tf_op jit(solution)/shard_map/broadcast_in_dim | solution.py:92
  23.8 3.8 %all-to-all-start.1 = ((bf16[4,4,256,256]{3,2,1,0:T(8,128)(2,1)}), bf16[4,4,256,256]{3,2,1,0:T(8,128)(2,1)S(1)}, u32[]{:S(2)}, u32[]{:S(2)}) async-start(bf16[4,4,256,256]{3,2,1,0:T(8,128)(2,1)} %broadcast_in_dim.17), calls=%async_computation.1 | async-start | bytes 4194304 | tf_op jit(solution)/shard_map/all_to_all | solution.py:91
  27.6 0.0 copy-done.3
  27.6 0.1 copy.52
  27.7 0.1 reduce-window.9
  27.8 0.1 reduce
  27.9 0.0 copy-done.1
  27.9 0.0 copy-done.2
  28.0 0.2 multiply_bitcast_fusion
  28.1 0.2 copy.66
  28.3 0.3 bitcast_reduce_fusion
  28.7 0.7 copy.57
  29.4 0.1 broadcast_multiply_fusion
  29.4 0.1 iota_add_fusion
  29.5 0.1 select_reduce_fusion
  29.6 0.1 slice_reduce_fusion
  29.7 0.6 subtract_maximum_fusion.kb0_ref
  30.3 21.3 %all-to-all-done.1 = bf16[4,4,256,256]{3,2,1,0:T(8,128)(2,1)S(1)} async-done(((bf16[4,4,256,256]{3,2,1,0:T(8,128)(2,1)}), bf16[4,4,256,256]{3,2,1,0:T(8,128)(2,1)S(1)}, u32[]{:S(2)}, u32[]{:S(2)}) %all-to-all-start.1) | async-done | bytes 2097184 | tf_op jit(solution)/shard_map/all_to_all | solution.py:91
  51.5 0.1 copy.53
  51.7 0.2 slice_bitcast_fusion
  51.9 0.0 copy-done.4
  51.9 0.1 reverse_bitcast_fusion
  52.0 0.3 pad_maximum_fusion
  52.3 0.2 constant_dynamic-slice_fusion.1
  52.4 0.8 copy.55
  53.3 0.8 copy.56
  54.1 1.1 fusion.2.kt_ref
  55.2 1.6 %pad_maximum_fusion.1 = bf16[2,17,128,256]{2,3,1,0:T(8,128)(2,1)} fusion(bf16[1,17,128,256]{2,3,1,0:T(8,128)(2,1)S(1)} %bitcast.38, bf16[1,17,128,256]{2,3,1,0:T(8,128)(2,1)S(1)} %bitcast.36), kind=kLoop, calls=%fused_computation.3 | loop fusion | flops 1114112 | bytes 4456448 | tf_op jit(solution)/shard_map/stack | solution.py:98
  56.8 4.1 %copy.58.kv_ref = bf16[2,17,128,256]{3,2,1,0:T(8,128)(2,1)} copy(bf16[2,17,128,256]{2,3,1,0:T(8,128)(2,1)} %pad_maximum_fusion.1) | data formatting | bytes 4456448 | tf_op jit(solution)/shard_map/stack | solution.py:98
  60.9 0.6 tile.18
  61.5 0.6 tile.16
  62.1 7.8 %shard_map.85 = (bf16[256,1024]{1,0:T(8,128)(2,1)}, f32[2,17,128,256]{3,2,1,0:T(8,128)}) custom-call(s32[2]{0:T(128)} %copy-done.4, s32[2]{0:T(128)} %subtract_maximum_fusion.kb0_ref, bf16[256,1024]{1,0:T(8,128)(2,1)} %q_ref.1, bf16[256,1024]{1,0:T(8,128)(2,1)} %do_ref.1, bf16[2,17,128,256]{3,2,1,0:T(8,128)(2,1)} %copy.58.kv_ref, ...), custom_call_target="tpu_custom_call" | custom-call | flops 6845104128 | bytes 8388608 | tf_op jit(solution)/shard_map/pallas_call | solution.py:142
  69.9 0.7 broadcast_in_dim.18
  70.6 1.5 %copy-done = f32[2,17,128,256]{3,2,1,0:T(8,128)S(1)} copy-done((f32[2,17,128,256]{3,2,1,0:T(8,128)S(1)}, f32[2,17,128,256]{3,2,1,0:T(8,128)}, u32[]{:S(2)}) %copy-start) | copy-done | bytes 4456472
  72.1 0.2 bitcast_dynamic-update-slice_fusion
  72.4 0.5 fusion
  72.9 0.3 fusion.3
  73.2 0.1 rev.10
  73.2 0.2 pad_maximum_fusion.2
  73.5 0.2 copy.63
  73.7 29.0 %all_to_all.21 = bf16[4,4,2,128,256]{4,3,0,2,1:T(8,128)(2,1)S(1)} all-to-all(bf16[4,4,2,128,256]{4,3,0,2,1:T(8,128)(2,1)S(1)} %copy.63), channel_id=1, replica_groups=mesh['zp'=4,'w'=4,'grp'=2] {'w'}, dimensions={1} | all-to-all | bytes 4194304 | tf_op jit(solution)/shard_map/all_to_all | solution.py:162
  102.7 0.3 convert_reduce_fusion
  103.1 0.1 copy.62
  103.2 44.1 %all_to_all.22 = f32[4,2,128,256]{3,2,1,0:T(8,128)S(1)} all-to-all(f32[4,2,128,256]{3,2,1,0:T(8,128)S(1)} %copy.62), channel_id=1, replica_groups=mesh['zp'=4,'w'=4,'grp'=2] {'zp'}, dimensions={0} | all-to-all | bytes 2097152 | tf_op jit(solution)/shard_map/all_to_all | solution.py:164
  147.3 0.1 reduce_sum.29
  147.4 0.7 fusion.4
  (9 shorter events, 0.1 us)
Async XLA Ops:
  23.8 3.9 %copy-start.3 = (s32[64]{0:T(128)S(1)}, s32[64]{0:T(128)}, u32[]{:S(2)}) copy-start(s32[64]{0:T(128)} %param.11) | copy-start | bytes 772
  23.8 4.2 %copy-start.1 = (bf16[256,1024]{1,0:T(8,128)(2,1)S(1)}, bf16[256,1024]{1,0:T(8,128)(2,1)}, u32[]{:S(2)}) copy-start(bf16[256,1024]{1,0:T(8,128)(2,1)} %param.9) | copy-start | bytes 1572868
  23.8 4.2 %copy-start.2 = (bf16[256,1024]{1,0:T(8,128)(2,1)S(1)}, bf16[256,1024]{1,0:T(8,128)(2,1)}, u32[]{:S(2)}) copy-start(bf16[256,1024]{1,0:T(8,128)(2,1)} %do_ref.1) | copy-start | bytes 1572868
  23.8 27.8 %all-to-all-start.1 = ((bf16[4,4,256,256]{3,2,1,0:T(8,128)(2,1)}), bf16[4,4,256,256]{3,2,1,0:T(8,128)(2,1)S(1)}, u32[]{:S(2)}, u32[]{:S(2)}) async-start(bf16[4,4,256,256]{3,2,1,0:T(8,128)(2,1)} %broadcast_in_dim.17), calls=%async_computation.1 | async-start | bytes 4194304 | tf_op jit(solution)/shard_map/all_to_all | solution.py:91
  29.4 22.4 %copy-start.4 = (s32[2]{0:T(128)}, s32[2]{0:T(128)S(1)}, u32[]{:S(2)}) copy-start(s32[2]{0:T(128)S(1)} %get-tuple-element.8.blk_ref) | copy-start | bytes 28
  69.9 2.3 %copy-start = (f32[2,17,128,256]{3,2,1,0:T(8,128)S(1)}, f32[2,17,128,256]{3,2,1,0:T(8,128)}, u32[]{:S(2)}) copy-start(f32[2,17,128,256]{3,2,1,0:T(8,128)} %get-tuple-element.6) | copy-start | bytes 13369348
where the time goes:
time: 146 us; the launch traced here: 148 us
  blocking collectives  93.8 us (64%)
  waiting for transfers between devices  21.3 us (15%)
  local copies, waits for them, and re-layouts  14.1 us (10%)
  Pallas kernels  7.75 us (5%)
  other arithmetic  6.41 us (4%)
  starting transfers between devices  3.85 us (3%)
    all_to_all x1, blocking collectives, body(): column = lax.all_to_all(plane, 'zp', 0, 0)  44.1 us
    all_to_all x1, blocking collectives, body(): plane = lax.all_to_all(storage, 'w', 1, 1)  29 us
    all_to_all x1, waiting for transfers between devices, body(): lax.all_to_all(jnp.broadcast_to(kv_col[None], (n_in,) + kv_col.shape), 'w...  21.3 us
    all_to_all x1, blocking collectives, body(): lax.all_to_all(jnp.broadcast_to(kv_local[None], (n_out,) + kv_local.shape...  20.6 us
    pallas_call x1, Pallas kernels, body(): pl.pallas_call(kernel, grid_spec=grid_spec, out_shape=[jax.ShapeDtypeStru...  7.75 us
    another operation x1, local copies, waits for them, and re-layouts, body(): jnp.stack([lax.dynamic_slice_in_dim(kv_seq, blocks[i], win, 0) for i in r...  4.14 us
    all_to_all x1, starting transfers between devices, body(): lax.all_to_all(jnp.broadcast_to(kv_col[None], (n_in,) + kv_col.shape), 'w...  3.85 us
  transfers between devices with their start and end apart: 1, of which 1 were waited for; matrix products, arithmetic and copies ran while one was open for 2% of the time, Pallas kernels for 0%

commit v1 on v0

--- a/solution.py
+++ b/solution.py
@@ -161,8 +161,8 @@
     storage = storage.reshape(n_out, n_in, 2, rows, 2 * width).astype(jnp.bfloat16)
     plane = lax.all_to_all(storage, "w", 1, 1)
     plane = jnp.sum(plane.astype(jnp.float32), axis=1)
-    column = lax.all_to_all(plane, "zp", 0, 0)
-    summed = jnp.sum(column, axis=0).reshape(2 * rows, 2 * width)
+    column = lax.all_to_all(plane.astype(jnp.bfloat16), "zp", 0, 0)
+    summed = jnp.sum(column.astype(jnp.float32), axis=0).reshape(2 * rows, 2 * width)
     grad_keys = summed[:, :width].astype(jnp.bfloat16)
     grad_values = summed[:, width:].astype(jnp.bfloat16)
     return (grad_queries, grad_keys, grad_values)

time: 146 us -> 132 us (0.904); the launches traced: 148 us -> 133 us
  blocking collectives: 93.8 us -> 78.3 us
    all_to_all x1, blocking collectives: 44.1 us -> 29.7 us  [body(): column = lax.all_to_all(plane.astype(jnp.bfloat16), 'zp', 0, 0)]
where the time goes in v1:
time: 132 us; the launch traced here: 133 us
  blocking collectives  78.3 us (59%)
  waiting for transfers between devices  21.3 us (16%)
  local copies, waits for them, and re-layouts  14 us (11%)
  Pallas kernels  7.75 us (6%)
  other arithmetic  6.46 us (5%)
  starting transfers between devices  3.85 us (3%)
    all_to_all x1, blocking collectives, body(): column = lax.all_to_all(plane.astype(jnp.bfloat16), 'zp', 0, 0)  29.7 us
    all_to_all x1, blocking collectives, body(): plane = lax.all_to_all(storage, 'w', 1, 1)  28 us
    all_to_all x1, waiting for transfers between devices, body(): lax.all_to_all(jnp.broadcast_to(kv_col[None], (n_in,) + kv_col.shape), 'w...  21.3 us
    all_to_all x1, blocking collectives, body(): lax.all_to_all(jnp.broadcast_to(kv_local[None], (n_out,) + kv_local.shape...  20.6 us
    pallas_call x1, Pallas kernels, body(): pl.pallas_call(kernel, grid_spec=grid_spec, out_shape=[jax.ShapeDtypeStru...  7.75 us
    another operation x1, local copies, waits for them, and re-layouts, body(): jnp.stack([lax.dynamic_slice_in_dim(kv_seq, blocks[i], win, 0) for i in r...  4.14 us
    all_to_all x1, starting transfers between devices, body(): lax.all_to_all(jnp.broadcast_to(kv_col[None], (n_in,) + kv_col.shape), 'w...  3.85 us
  transfers between devices with their start and end apart: 1, of which 1 were waited for; matrix products, arithmetic and copies ran while one was open for 2% of the time, Pallas kernels for 0%

profile of v1, /device:TPU:0, one launch (start us, length us, event | category | flops | bytes accessed | tf_op | source)
XLA Modules:
  0.0 132.5 jit_solution(3345311501694983931)
XLA Ops:
  0.6 0.9 pad_maximum_fusion.3
  1.6 20.6 %all_to_all.20 = bf16[4,256,256]{2,1,0:T(8,128)(2,1)S(1)} all-to-all(bf16[4,256,256]{2,1,0:T(8,128)(2,1)S(1)} %broadcast_in_dim.16), channel_id=1, replica_groups=mesh['zp'=4,'w'=4,'grp'=2] {'zp'}, dimensions={0} | all-to-all | bytes 1048576 | tf_op jit(solution)/shard_map/all_to_all | solution.py:88
  22.2 1.6 %broadcast_in_dim.17 = bf16[4,4,256,256]{3,2,1,0:T(8,128)(2,1)} broadcast(bf16[4,256,256]{2,1,0:T(8,128)(2,1)S(1)} %all_to_all.20), dimensions={1,2,3} | broadcast | bytes 2621440 | tf_op jit(solution)/shard_map/broadcast_in_dim | solution.py:92
  23.8 0.0 copy-start.3
  23.8 3.8 %all-to-all-start.1 = ((bf16[4,4,256,256]{3,2,1,0:T(8,128)(2,1)}), bf16[4,4,256,256]{3,2,1,0:T(8,128)(2,1)S(1)}, u32[]{:S(2)}, u32[]{:S(2)}) async-start(bf16[4,4,256,256]{3,2,1,0:T(8,128)(2,1)} %broadcast_in_dim.17), calls=%async_computation.1 | async-start | bytes 4194304 | tf_op jit(solution)/shard_map/all_to_all | solution.py:91
  27.6 0.0 copy-done.3
  27.6 0.1 copy.52
  27.7 0.1 reduce-window.9
  27.8 0.1 reduce.2
  27.9 0.0 copy-done.1
  27.9 0.0 copy-done.2
  28.0 0.2 multiply_bitcast_fusion
  28.1 0.2 copy.66
  28.3 0.3 bitcast_reduce_fusion
  28.7 0.7 copy.57
  29.4 0.1 broadcast_multiply_fusion
  29.4 0.1 iota_add_fusion
  29.5 0.1 select_reduce_fusion
  29.6 0.1 slice_reduce_fusion
  29.7 0.6 subtract_maximum_fusion.kb0_ref
  30.3 21.3 %all-to-all-done.1 = bf16[4,4,256,256]{3,2,1,0:T(8,128)(2,1)S(1)} async-done(((bf16[4,4,256,256]{3,2,1,0:T(8,128)(2,1)}), bf16[4,4,256,256]{3,2,1,0:T(8,128)(2,1)S(1)}, u32[]{:S(2)}, u32[]{:S(2)}) %all-to-all-start.1) | async-done | bytes 2097184 | tf_op jit(solution)/shard_map/all_to_all | solution.py:91
  51.5 0.1 copy.53
  51.7 0.2 slice_bitcast_fusion
  51.9 0.0 copy-done.4
  51.9 0.1 reverse_bitcast_fusion
  52.0 0.3 pad_maximum_fusion
  52.3 0.2 constant_dynamic-slice_fusion.1
  52.4 0.8 copy.55
  53.3 0.8 copy.56
  54.1 1.1 fusion.2.kt_ref
  55.2 1.6 %pad_maximum_fusion.1 = bf16[2,17,128,256]{2,3,1,0:T(8,128)(2,1)} fusion(bf16[1,17,128,256]{2,3,1,0:T(8,128)(2,1)S(1)} %bitcast.38, bf16[1,17,128,256]{2,3,1,0:T(8,128)(2,1)S(1)} %bitcast.36), kind=kLoop, calls=%fused_computation.2 | loop fusion | flops 1114112 | bytes 4456448 | tf_op jit(solution)/shard_map/stack | solution.py:98
  56.8 4.1 %copy.58.kv_ref = bf16[2,17,128,256]{3,2,1,0:T(8,128)(2,1)} copy(bf16[2,17,128,256]{2,3,1,0:T(8,128)(2,1)} %pad_maximum_fusion.1) | data formatting | bytes 4456448 | tf_op jit(solution)/shard_map/stack | solution.py:98
  60.9 0.6 tile.18
  61.5 0.6 tile.16
  62.1 7.8 %shard_map.85 = (bf16[256,1024]{1,0:T(8,128)(2,1)}, f32[2,17,128,256]{3,2,1,0:T(8,128)}) custom-call(s32[2]{0:T(128)} %copy-done.4, s32[2]{0:T(128)} %subtract_maximum_fusion.kb0_ref, bf16[256,1024]{1,0:T(8,128)(2,1)} %q_ref.1, bf16[256,1024]{1,0:T(8,128)(2,1)} %do_ref.1, bf16[2,17,128,256]{3,2,1,0:T(8,128)(2,1)} %copy.58.kv_ref, ...), custom_call_target="tpu_custom_call" | custom-call | flops 6845104128 | bytes 8388608 | tf_op jit(solution)/shard_map/pallas_call | solution.py:142
  69.9 0.7 broadcast_in_dim.18
  70.6 1.5 %copy-done = f32[2,17,128,256]{3,2,1,0:T(8,128)S(1)} copy-done((f32[2,17,128,256]{3,2,1,0:T(8,128)S(1)}, f32[2,17,128,256]{3,2,1,0:T(8,128)}, u32[]{:S(2)}) %copy-start) | copy-done | bytes 4456472
  72.1 0.2 bitcast_dynamic-update-slice_fusion
  72.4 0.5 fusion
  72.9 0.3 fusion.3
  73.2 0.1 rev.10
  73.2 0.2 pad_maximum_fusion.2
  73.5 0.2 copy.63
  73.7 28.0 %all_to_all.21 = bf16[4,4,2,128,256]{4,3,0,2,1:T(8,128)(2,1)S(1)} all-to-all(bf16[4,4,2,128,256]{4,3,0,2,1:T(8,128)(2,1)S(1)} %copy.63), channel_id=1, replica_groups=mesh['zp'=4,'w'=4,'grp'=2] {'w'}, dimensions={1} | all-to-all | bytes 4194304 | tf_op jit(solution)/shard_map/all_to_all | solution.py:162
  101.6 0.4 reduce_sum.31
  102.1 29.7 %all_to_all.22 = bf16[4,2,128,256]{3,2,1,0:T(8,128)(2,1)S(1)} all-to-all(bf16[4,2,128,256]{3,2,1,0:T(8,128)(2,1)S(1)} %copy.62), channel_id=1, replica_groups=mesh['zp'=4,'w'=4,'grp'=2] {'zp'}, dimensions={0} | all-to-all | bytes 1048576 | tf_op jit(solution)/shard_map/all_to_all | solution.py:164
  131.8 0.1 reduce.1
  131.9 0.7 fusion.4
  (9 shorter events, 0.1 us)
Async XLA Ops:
  23.8 3.9 %copy-start.3 = (s32[64]{0:T(128)S(1)}, s32[64]{0:T(128)}, u32[]{:S(2)}) copy-start(s32[64]{0:T(128)} %param.11) | copy-start | bytes 772
  23.8 4.2 %copy-start.1 = (bf16[256,1024]{1,0:T(8,128)(2,1)S(1)}, bf16[256,1024]{1,0:T(8,128)(2,1)}, u32[]{:S(2)}) copy-start(bf16[256,1024]{1,0:T(8,128)(2,1)} %param.9) | copy-start | bytes 1572868
  23.8 4.2 %copy-start.2 = (bf16[256,1024]{1,0:T(8,128)(2,1)S(1)}, bf16[256,1024]{1,0:T(8,128)(2,1)}, u32[]{:S(2)}) copy-start(bf16[256,1024]{1,0:T(8,128)(2,1)} %do_ref.1) | copy-start | bytes 1572868
  23.8 27.8 %all-to-all-start.1 = ((bf16[4,4,256,256]{3,2,1,0:T(8,128)(2,1)}), bf16[4,4,256,256]{3,2,1,0:T(8,128)(2,1)S(1)}, u32[]{:S(2)}, u32[]{:S(2)}) async-start(bf16[4,4,256,256]{3,2,1,0:T(8,128)(2,1)} %broadcast_in_dim.17), calls=%async_computation.1 | async-start | bytes 4194304 | tf_op jit(solution)/shard_map/all_to_all | solution.py:91
  29.4 22.4 %copy-start.4 = (s32[2]{0:T(128)}, s32[2]{0:T(128)S(1)}, u32[]{:S(2)}) copy-start(s32[2]{0:T(128)S(1)} %get-tuple-element.8.blk_ref) | copy-start | bytes 28
  69.9 2.3 %copy-start = (f32[2,17,128,256]{3,2,1,0:T(8,128)S(1)}, f32[2,17,128,256]{3,2,1,0:T(8,128)}, u32[]{:S(2)}) copy-start(f32[2,17,128,256]{3,2,1,0:T(8,128)} %get-tuple-element.6) | copy-start | bytes 13369348

commit v2 on v1

--- a/solution.py
+++ b/solution.py
@@ -70,6 +70,26 @@
         dq_ref[:, h * width:(h + 1) * width] = (piece.T * scaling).astype(jnp.bfloat16)
 
 
+def _shift(x, k, n, axis):
+    return lax.ppermute(x, axis, [(i, (i + k) % n) for i in range(n)])
+
+
+def _group_gather(x, n, axis):
+    me = lax.axis_index(axis)
+    got = jnp.stack([x] + [_shift(x, k, n, axis) for k in range(1, n)])
+    order = (me - jnp.arange(n)) % n
+    return jnp.take(got, order, axis=0)
+
+
+def _group_reduce(parts, n, axis, dim):
+    me = lax.axis_index(axis)
+    total = lax.dynamic_index_in_dim(parts, me, dim, keepdims=False).astype(jnp.float32)
+    for k in range(1, n):
+        piece = lax.dynamic_index_in_dim(parts, (me + k) % n, dim, keepdims=False)
+        total = total + _shift(piece.astype(jnp.bfloat16), k, n, axis).astype(jnp.float32)
+    return total
+
+
 def body(queries, shared_keys, shared_values, outputs, out_grad, doc_lengths):
     n_in = lax.axis_size("w")
     rank = lax.axis_index("zp") * n_in + lax.axis_index("w")
@@ -85,12 +105,8 @@
     blocks = jnp.stack([rank, 2 * n_seq - 1 - rank]).astype(jnp.int32)
 
     kv_local = jnp.concatenate([shared_keys, shared_values], axis=1)
-    kv_col = lax.all_to_all(
-        jnp.broadcast_to(kv_local[None], (n_out,) + kv_local.shape), "zp", 0, 0
-    )
-    kv_all = lax.all_to_all(
-        jnp.broadcast_to(kv_col[None], (n_in,) + kv_col.shape), "w", 0, 0
-    )
+    kv_col = _group_gather(kv_local, n_out, "zp")
+    kv_all = _group_gather(kv_col, n_in, "w")
     kv_st = jnp.swapaxes(kv_all, 0, 1).reshape(n_seq, 2, rows, 2 * width)
     kv_seq = jnp.concatenate(
         [jnp.zeros((REACH, rows, 2 * width), kv_all.dtype), kv_st[:, 0], kv_st[::-1, 1]], axis=0
@@ -159,10 +175,8 @@
     acc = acc[REACH:]
     storage = jnp.stack([acc[:n_seq], acc[n_seq:][::-1]], axis=1)
     storage = storage.reshape(n_out, n_in, 2, rows, 2 * width).astype(jnp.bfloat16)
-    plane = lax.all_to_all(storage, "w", 1, 1)
-    plane = jnp.sum(plane.astype(jnp.float32), axis=1)
-    column = lax.all_to_all(plane.astype(jnp.bfloat16), "zp", 0, 0)
-    summed = jnp.sum(column.astype(jnp.float32), axis=0).reshape(2 * rows, 2 * width)
+    plane = _group_reduce(storage, n_in, "w", 1)
+    summed = _group_reduce(plane, n_out, "zp", 0).reshape(2 * rows, 2 * width)
     grad_keys = summed[:, :width].astype(jnp.bfloat16)
     grad_values = summed[:, width:].astype(jnp.bfloat16)
     return (grad_queries, grad_keys, grad_values)

time: 132 us -> 140 us (1.061); the launches traced: 133 us -> 138 us
  blocking collectives: 78.3 us -> 0 us
  starting transfers between devices: 3.85 us -> 44.4 us
  waiting for transfers between devices: 21.3 us -> 54.5 us
  other arithmetic: 6.46 us -> 12.5 us
  local copies, waits for them, and re-layouts: 14 us -> 18.3 us
    all_to_all x3 -> x0, blocking collectives: 78.3 us -> none  [the longest x1 29.7 us: body(): column = lax.all_to_all(plane.astype(jnp.bfloat16), 'zp', 0, 0)]
    ppermute x0 -> x12, waiting for transfers between devices: none -> 54.5 us  [_shift(): return lax.ppermute(x, axis, [(i, (i + k) % n) for i in range(n)])]
    ppermute x0 -> x12, starting transfers between devices: none -> 44.4 us  [_shift(): return lax.ppermute(x, axis, [(i, (i + k) % n) for i in range(n)])]
    all_to_all x1 -> x0, waiting for transfers between devices: 21.3 us -> none  [body(): lax.all_to_all(jnp.broadcast_to(kv_col[None], (n_in,) + kv_col.shape), 'w...]
    all_to_all x1 -> x0, starting transfers between devices: 3.85 us -> none  [body(): lax.all_to_all(jnp.broadcast_to(kv_col[None], (n_in,) + kv_col.shape), 'w...]
    gather x0 -> x2, local copies, waits for them, and re-layouts: none -> 2.59 us  [_group_gather(): return jnp.take(got, order, axis=0)]
    unnamed x11 -> x14, local copies, waits for them, and re-layouts: 1.73 us -> 4.26 us
    select_n x0 -> x5, other arithmetic: none -> 2.11 us  [_group_gather(): return jnp.take(got, order, axis=0)]
  transfers between devices with their start and end apart: 1 -> 12, of which waited for: 1 -> 9; matrix products, arithmetic and copies ran while one was open for 2% -> 3% of each run, Pallas kernels for 0% -> 0%
where the time goes in v2:
time: 140 us; the launch traced here: 138 us
  waiting for transfers between devices  54.5 us (39%)
  starting transfers between devices  44.4 us (32%)
  local copies, waits for them, and re-layouts  18.3 us (13%)
  other arithmetic  12.5 us (9%)
  Pallas kernels  7.74 us (6%)
    ppermute x12, waiting for transfers between devices, _shift(): return lax.ppermute(x, axis, [(i, (i + k) % n) for i in range(n)])  54.5 us
    ppermute x12, starting transfers between devices, _shift(): return lax.ppermute(x, axis, [(i, (i + k) % n) for i in range(n)])  44.4 us
    pallas_call x1, Pallas kernels, body(): pl.pallas_call(kernel, grid_spec=grid_spec, out_shape=[jax.ShapeDtypeStru...  7.74 us
    unnamed x14, local copies, waits for them, and re-layouts  4.26 us
    another operation x1, local copies, waits for them, and re-layouts, body(): jnp.stack([lax.dynamic_slice_in_dim(kv_seq, blocks[i], win, 0) for i in r...  4.16 us
  transfers between devices with their start and end apart: 12, of which 9 were waited for; matrix products, arithmetic and copies ran while one was open for 3% of the time, Pallas kernels for 0%

profile of v2, /device:TPU:0, one launch (start us, length us, event | category | flops | bytes accessed | tf_op | source)
XLA Modules:
  0.0 138.3 jit_solution(3851749260144620187)
XLA Ops:
  0.6 0.9 constant_dynamic-update-slice_fusion.1
  1.5 0.9 constant_dynamic-update-slice_fusion
  2.3 3.1 %collective-permute-start = (bf16[256,256]{1,0:T(8,128)(2,1)S(1)}, bf16[256,256]{1,0:T(8,128)(2,1)S(1)}, u32[]{:S(2)}, u32[]{:S(2)}) collective-permute-start(bf16[256,256]{1,0:T(8,128)(2,1)S(1)} %constant_dynamic-update-slice_fusion), channel_id=1, source_target_pairs={{0,8},{8,16},{16,24},{24,0},{1,9},{9,17},{17,25},{25,1},{2,10},{10... | collective-permute-start | bytes 393224 | tf_op jit(solution)/shard_map/ppermute | solution.py:74
  5.5 2.6 %collective-permute-start.1 = (bf16[256,256]{1,0:T(8,128)(2,1)S(1)}, bf16[256,256]{1,0:T(8,128)(2,1)S(1)}, u32[]{:S(2)}, u32[]{:S(2)}) collective-permute-start(bf16[256,256]{1,0:T(8,128)(2,1)S(1)} %constant_dynamic-update-slice_fusion), channel_id=1, source_target_pairs={{0,16},{8,24},{16,0},{24,8},{1,17},{9,25},{17,1},{25,9},{2,18},{10... | collective-permute-start | bytes 393224 | tf_op jit(solution)/shard_map/ppermute | solution.py:74
  8.0 1.3 collective-permute-start.2
  9.6 1.4 multiply_bitcast_fusion
  11.2 0.3 bitcast_reduce_fusion
  12.1 4.6 %collective-permute-done.1 = bf16[256,256]{1,0:T(8,128)(2,1)S(1)} collective-permute-done((bf16[256,256]{1,0:T(8,128)(2,1)S(1)}, bf16[256,256]{1,0:T(8,128)(2,1)S(1)}, u32[]{:S(2)}, u32[]{:S(2)}) %collective-permute-start.1) | collective-permute-done | bytes 131104 | tf_op jit(solution)/shard_map/ppermute | solution.py:74
  16.8 0.6 gather_fusion
  17.5 1.6 %collective-permute-start.4 = (bf16[4,256,256]{2,1,0:T(8,128)(2,1)S(1)}, bf16[4,256,256]{2,1,0:T(8,128)(2,1)S(1)}, u32[]{:S(2)}, u32[]{:S(2)}) collective-permute-start(bf16[4,256,256]{2,1,0:T(8,128)(2,1)S(1)} %broadcast_select_fusion), channel_id=1, source_target_pairs={{0,4},{2,6},{4,0},{6,2},{1,5},{3,7},{5,1},{7,3},{8,12},{10,14},{12... | collective-permute-start | bytes 1572872 | tf_op jit(solution)/shard_map/ppermute | solution.py:74
  19.1 1.4 %collective-permute-start.5 = (bf16[4,256,256]{2,1,0:T(8,128)(2,1)S(1)}, bf16[4,256,256]{2,1,0:T(8,128)(2,1)S(1)}, u32[]{:S(2)}, u32[]{:S(2)}) collective-permute-start(bf16[4,256,256]{2,1,0:T(8,128)(2,1)S(1)} %broadcast_select_fusion), channel_id=1, source_target_pairs={{0,6},{2,0},{4,2},{6,4},{1,7},{3,1},{5,3},{7,5},{8,14},{10,8},{12,... | collective-permute-start | bytes 1572872 | tf_op jit(solution)/shard_map/ppermute | solution.py:74
  20.5 0.6 collective-permute-start.3
  21.2 0.7 copy.55
  21.9 0.6 subtract_maximum_fusion.kb0_ref
  22.6 8.8 %collective-permute-done.4 = bf16[4,256,256]{2,1,0:T(8,128)(2,1)S(1)} collective-permute-done((bf16[4,256,256]{2,1,0:T(8,128)(2,1)S(1)}, bf16[4,256,256]{2,1,0:T(8,128)(2,1)S(1)}, u32[]{:S(2)}, u32[]{:S(2)}) %collective-permute-start.4) | collective-permute-done | bytes 524320 | tf_op jit(solution)/shard_map/ppermute | solution.py:74
  31.4 2.4 %collective-permute-done.5 = bf16[4,256,256]{2,1,0:T(8,128)(2,1)S(1)} collective-permute-done((bf16[4,256,256]{2,1,0:T(8,128)(2,1)S(1)}, bf16[4,256,256]{2,1,0:T(8,128)(2,1)S(1)}, u32[]{:S(2)}, u32[]{:S(2)}) %collective-permute-start.5) | collective-permute-done | bytes 524320 | tf_op jit(solution)/shard_map/ppermute | solution.py:74
  33.9 9.9 %collective-permute-done.3 = bf16[4,256,256]{2,1,0:T(8,128)(2,1)S(1)} collective-permute-done((bf16[4,256,256]{2,1,0:T(8,128)(2,1)S(1)}, bf16[4,256,256]{2,1,0:T(8,128)(2,1)S(1)}, u32[]{:S(2)}, u32[]{:S(2)}) %collective-permute-start.3) | collective-permute-done | bytes 524320 | tf_op jit(solution)/shard_map/ppermute | solution.py:74
  43.7 0.8 copy-done.3
  44.5 1.3 pad_maximum_fusion.2
  45.8 2.0 %gather_fusion.1 = bf16[4,4,256,256]{3,2,1,0:T(8,128)(2,1)} fusion(bf16[4,4,256,256]{3,2,1,0:T(8,128)(2,1)S(1)} %pad_maximum_fusion.2, s32[1024]{0:T(1024)S(1)} %pad_clamp_fusion), kind=kCustom, calls=%fused_computation.1 | custom fusion | bytes 4194320 | tf_op jit(solution)/shard_map/jit(_take)/gather | solution.py:81
  47.8 1.9 %select_bitcast_fusion = bf16[4,4,256,256]{3,2,0,1:T(8,128)(2,1)S(1)} fusion(bf16[4,4,256,256]{3,2,1,0:T(8,128)(2,1)} %gather_fusion.1, pred[4]{0:T(512)(128)(4,1)S(1)} %get-tuple-element.24), kind=kLoop, calls=%fused_computation.20 | loop fusion | flops 1048576 | bytes 4194308 | tf_op jit(solution)/shard_map/jit(_take)/select_n | solution.py:81
  50.1 0.3 pad_maximum_fusion
  50.6 0.8 copy.53
  51.4 0.8 copy.54
  52.3 1.1 fusion.2.kt_ref
  53.4 1.6 %pad_maximum_fusion.1 = bf16[2,17,128,256]{2,3,1,0:T(8,128)(2,1)} fusion(bf16[1,17,128,256]{2,3,1,0:T(8,128)(2,1)S(1)} %bitcast.84, bf16[1,17,128,256]{2,3,1,0:T(8,128)(2,1)S(1)} %bitcast.82), kind=kLoop, calls=%fused_computation.12 | loop fusion | flops 1114112 | bytes 4456448 | tf_op jit(solution)/shard_map/stack | solution.py:114
  54.9 4.2 %copy.56.kv_ref = bf16[2,17,128,256]{3,2,1,0:T(8,128)(2,1)} copy(bf16[2,17,128,256]{2,3,1,0:T(8,128)(2,1)} %pad_maximum_fusion.1) | data formatting | bytes 4456448 | tf_op jit(solution)/shard_map/stack | solution.py:114
  59.1 0.6 tile.16
  59.7 0.6 tile.18
  60.3 7.7 %shard_map.85 = (bf16[256,1024]{1,0:T(8,128)(2,1)}, f32[2,17,128,256]{3,2,1,0:T(8,128)}) custom-call(s32[2]{0:T(128)} %copy-done.5, s32[2]{0:T(128)} %subtract_maximum_fusion.kb0_ref, bf16[256,1024]{1,0:T(8,128)(2,1)} %q_ref.1, bf16[256,1024]{1,0:T(8,128)(2,1)} %do_ref.1, bf16[2,17,128,256]{3,2,1,0:T(8,128)(2,1)} %copy.56.kv_ref, ...), custom_call_target="tpu_custom_call" | custom-call | flops 6845104128 | bytes 8388608 | tf_op jit(solution)/shard_map/pallas_call | solution.py:158
  68.1 0.7 broadcast_in_dim.53
  68.8 1.5 %copy-done = f32[2,17,128,256]{3,2,1,0:T(8,128)S(1)} copy-done((f32[2,17,128,256]{3,2,1,0:T(8,128)S(1)}, f32[2,17,128,256]{3,2,1,0:T(8,128)}, u32[]{:S(2)}) %copy-start) | copy-done | bytes 4456472
  70.6 0.5 fusion
  71.0 0.3 fusion.25
  71.4 1.2 fusion.10
  72.6 4.7 %collective-permute-start.6 = (bf16[4,2,128,256]{3,2,0,1:T(8,128)(2,1)}, bf16[4,2,128,256]{3,2,0,1:T(8,128)(2,1)S(1)}, u32[]{:S(2)}, u32[]{:S(2)}) collective-permute-start(bf16[4,2,128,256]{3,2,0,1:T(8,128)(2,1)} %get-tuple-element.13), channel_id=1, source_target_pairs={{0,2},{2,4},{4,6},{6,0},{1,3},{3,5},{5,7},{7,1},{8,10},{10,12},{12... | collective-permute-start | bytes 1572872 | tf_op jit(solution)/shard_map/ppermute | solution.py:74
  77.4 1.8 %collective-permute-start.8 = (bf16[4,2,128,256]{3,2,0,1:T(8,128)(2,1)}, bf16[4,2,128,256]{3,2,0,1:T(8,128)(2,1)}, u32[]{:S(2)}, u32[]{:S(2)}) collective-permute-start(bf16[4,2,128,256]{3,2,0,1:T(8,128)(2,1)} %get-tuple-element.15), channel_id=1, source_target_pairs={{0,6},{2,0},{4,2},{6,4},{1,7},{3,1},{5,3},{7,5},{8,14},{10,8},{12,... | collective-permute-start | bytes 1572872 | tf_op jit(solution)/shard_map/ppermute | solution.py:74
  79.2 10.8 %collective-permute-done.6 = bf16[4,2,128,256]{3,2,0,1:T(8,128)(2,1)S(1)} collective-permute-done((bf16[4,2,128,256]{3,2,0,1:T(8,128)(2,1)}, bf16[4,2,128,256]{3,2,0,1:T(8,128)(2,1)S(1)}, u32[]{:S(2)}, u32[]{:S(2)}) %collective-permute-start.6) | collective-permute-done | bytes 524320 | tf_op jit(solution)/shard_map/ppermute | solution.py:74
  90.0 8.9 %collective-permute-done.7 = bf16[4,2,128,256]{3,2,0,1:T(8,128)(2,1)S(1)} collective-permute-done((bf16[4,2,128,256]{3,2,0,1:T(8,128)(2,1)}, bf16[4,2,128,256]{3,2,0,1:T(8,128)(2,1)S(1)}, u32[]{:S(2)}, u32[]{:S(2)}) %collective-permute-start.7) | collective-permute-done | bytes 524320 | tf_op jit(solution)/shard_map/ppermute | solution.py:74
  98.9 0.8 copy-done.2
  99.7 0.2 collective-permute-done.8
  99.9 1.6 %fusion.4 = f32[4,2,128,256]{3,2,0,1:T(8,128)S(1)} fusion(bf16[4,2,128,256]{3,2,0,1:T(8,128)(2,1)} %collective-permute-done.8, bf16[4,2,128,256]{3,2,0,1:T(8,128)(2,1)} %copy-done.2, bf16[4,2,128,256]{3,2,0,1:T(8,128)(2,1)} %copy-done.1, s32[]{:T(128)S(6)} %select_n.171, bf16[4,4,1,128,256]{4,3,1,0,2:T(8,128)(2,1)S(1)} %bitcast.88, ...), kind=kLoop, calls=%fused_computation.27 | loop fusion | flops 2097152 | bytes 4718596 | tf_op jit(solution)/shard_map/add | solution.py:89
  101.6 9.4 %collective-permute-start.10 = (bf16[2,128,256]{2,1,0:T(8,128)(2,1)S(1)}, bf16[2,128,256]{2,1,0:T(8,128)(2,1)S(1)}, u32[]{:S(2)}, u32[]{:S(2)}) collective-permute-start(bf16[2,128,256]{2,1,0:T(8,128)(2,1)S(1)} %get-tuple-element.20), channel_id=1, source_target_pairs={{0,16},{8,24},{16,0},{24,8},{1,17},{9,25},{17,1},{25,9},{2,18},{10... | collective-permute-start | bytes 393224 | tf_op jit(solution)/shard_map/ppermute | solution.py:74
  111.0 17.2 %collective-permute-start.11 = (bf16[2,128,256]{2,1,0:T(8,128)(2,1)S(1)}, bf16[2,128,256]{2,1,0:T(8,128)(2,1)S(1)}, u32[]{:S(2)}, u32[]{:S(2)}) collective-permute-start(bf16[2,128,256]{2,1,0:T(8,128)(2,1)S(1)} %get-tuple-element.19), channel_id=1, source_target_pairs={{0,24},{8,0},{16,8},{24,16},{1,25},{9,1},{17,9},{25,17},{2,26},{10... | collective-permute-start | bytes 393224 | tf_op jit(solution)/shard_map/ppermute | solution.py:74
  128.2 0.5 collective-permute-start.9
  128.7 3.5 %collective-permute-done.11 = bf16[2,128,256]{2,1,0:T(8,128)(2,1)S(1)} collective-permute-done((bf16[2,128,256]{2,1,0:T(8,128)(2,1)S(1)}, bf16[2,128,256]{2,1,0:T(8,128)(2,1)S(1)}, u32[]{:S(2)}, u32[]{:S(2)}) %collective-permute-start.11) | collective-permute-done | bytes 131104 | tf_op jit(solution)/shard_map/ppermute | solution.py:74
  132.2 5.3 %collective-permute-done.9 = bf16[2,128,256]{2,1,0:T(8,128)(2,1)S(1)} collective-permute-done((bf16[2,128,256]{2,1,0:T(8,128)(2,1)S(1)}, bf16[2,128,256]{2,1,0:T(8,128)(2,1)S(1)}, u32[]{:S(2)}, u32[]{:S(2)}) %collective-permute-start.9) | collective-permute-done | bytes 131104 | tf_op jit(solution)/shard_map/ppermute | solution.py:74
  137.6 0.7 fusion.26
  (40 shorter events, 2.4 us)
Async XLA Ops:
  2.3 9.7 %collective-permute-start = (bf16[256,256]{1,0:T(8,128)(2,1)S(1)}, bf16[256,256]{1,0:T(8,128)(2,1)S(1)}, u32[]{:S(2)}, u32[]{:S(2)}) collective-permute-start(bf16[256,256]{1,0:T(8,128)(2,1)S(1)} %constant_dynamic-update-slice_fusion), channel_id=1, source_target_pairs={{0,8},{8,16},{16,24},{24,0},{1,9},{9,17},{17,25},{25,1},{2,10},{10... | collective-permute-start | bytes 393224 | tf_op jit(solution)/shard_map/ppermute | solution.py:74
  5.5 11.2 %collective-permute-start.1 = (bf16[256,256]{1,0:T(8,128)(2,1)S(1)}, bf16[256,256]{1,0:T(8,128)(2,1)S(1)}, u32[]{:S(2)}, u32[]{:S(2)}) collective-permute-start(bf16[256,256]{1,0:T(8,128)(2,1)S(1)} %constant_dynamic-update-slice_fusion), channel_id=1, source_target_pairs={{0,16},{8,24},{16,0},{24,8},{1,17},{9,25},{17,1},{25,9},{2,18},{10... | collective-permute-start | bytes 393224 | tf_op jit(solution)/shard_map/ppermute | solution.py:74
  8.0 8.6 %collective-permute-start.2 = (bf16[256,256]{1,0:T(8,128)(2,1)S(1)}, bf16[256,256]{1,0:T(8,128)(2,1)S(1)}, u32[]{:S(2)}, u32[]{:S(2)}) collective-permute-start(bf16[256,256]{1,0:T(8,128)(2,1)S(1)} %constant_dynamic-update-slice_fusion), channel_id=1, source_target_pairs={{0,24},{8,0},{16,8},{24,16},{1,25},{9,1},{17,9},{25,17},{2,26},{10... | collective-permute-start | bytes 393224 | tf_op jit(solution)/shard_map/ppermute | solution.py:74
  9.5 12.4 %copy-start.5 = (s32[2]{0:T(128)}, s32[2]{0:T(128)S(1)}, u32[]{:S(2)}) copy-start(s32[2]{0:T(128)S(1)} %get-tuple-element.8.blk_ref) | copy-start | bytes 28
  11.0 0.7 copy-start.4
  17.5 14.0 %collective-permute-start.4 = (bf16[4,256,256]{2,1,0:T(8,128)(2,1)S(1)}, bf16[4,256,256]{2,1,0:T(8,128)(2,1)S(1)}, u32[]{:S(2)}, u32[]{:S(2)}) collective-permute-start(bf16[4,256,256]{2,1,0:T(8,128)(2,1)S(1)} %broadcast_select_fusion), channel_id=1, source_target_pairs={{0,4},{2,6},{4,0},{6,2},{1,5},{3,7},{5,1},{7,3},{8,12},{10,14},{12... | collective-permute-start | bytes 1572872 | tf_op jit(solution)/shard_map/ppermute | solution.py:74
  19.1 14.8 %collective-permute-start.5 = (bf16[4,256,256]{2,1,0:T(8,128)(2,1)S(1)}, bf16[4,256,256]{2,1,0:T(8,128)(2,1)S(1)}, u32[]{:S(2)}, u32[]{:S(2)}) collective-permute-start(bf16[4,256,256]{2,1,0:T(8,128)(2,1)S(1)} %broadcast_select_fusion), channel_id=1, source_target_pairs={{0,6},{2,0},{4,2},{6,4},{1,7},{3,1},{5,3},{7,5},{8,14},{10,8},{12,... | collective-permute-start | bytes 1572872 | tf_op jit(solution)/shard_map/ppermute | solution.py:74
  20.5 23.2 %collective-permute-start.3 = (bf16[4,256,256]{2,1,0:T(8,128)(2,1)S(1)}, bf16[4,256,256]{2,1,0:T(8,128)(2,1)S(1)}, u32[]{:S(2)}, u32[]{:S(2)}) collective-permute-start(bf16[4,256,256]{2,1,0:T(8,128)(2,1)S(1)} %broadcast_select_fusion), channel_id=1, source_target_pairs={{0,2},{2,4},{4,6},{6,0},{1,3},{3,5},{5,7},{7,1},{8,10},{10,12},{12... | collective-permute-start | bytes 1572872 | tf_op jit(solution)/shard_map/ppermute | solution.py:74
  43.7 0.8 copy-start.3
  68.1 2.3 %copy-start = (f32[2,17,128,256]{3,2,1,0:T(8,128)S(1)}, f32[2,17,128,256]{3,2,1,0:T(8,128)}, u32[]{:S(2)}) copy-start(f32[2,17,128,256]{3,2,1,0:T(8,128)} %get-tuple-element.6) | copy-start | bytes 13369348
  72.6 17.4 %collective-permute-start.6 = (bf16[4,2,128,256]{3,2,0,1:T(8,128)(2,1)}, bf16[4,2,128,256]{3,2,0,1:T(8,128)(2,1)S(1)}, u32[]{:S(2)}, u32[]{:S(2)}) collective-permute-start(bf16[4,2,128,256]{3,2,0,1:T(8,128)(2,1)} %get-tuple-element.13), channel_id=1, source_target_pairs={{0,2},{2,4},{4,6},{6,0},{1,3},{3,5},{5,7},{7,1},{8,10},{10,12},{12... | collective-permute-start | bytes 1572872 | tf_op jit(solution)/shard_map/ppermute | solution.py:74
  77.4 21.5 %collective-permute-start.7 = (bf16[4,2,128,256]{3,2,0,1:T(8,128)(2,1)}, bf16[4,2,128,256]{3,2,0,1:T(8,128)(2,1)S(1)}, u32[]{:S(2)}, u32[]{:S(2)}) collective-permute-start(bf16[4,2,128,256]{3,2,0,1:T(8,128)(2,1)} %get-tuple-element.14), channel_id=1, source_target_pairs={{0,4},{2,6},{4,0},{6,2},{1,5},{3,7},{5,1},{7,3},{8,12},{10,14},{12... | collective-permute-start | bytes 1572872 | tf_op jit(solution)/shard_map/ppermute | solution.py:74
  77.4 22.6 %collective-permute-start.8 = (bf16[4,2,128,256]{3,2,0,1:T(8,128)(2,1)}, bf16[4,2,128,256]{3,2,0,1:T(8,128)(2,1)}, u32[]{:S(2)}, u32[]{:S(2)}) collective-permute-start(bf16[4,2,128,256]{3,2,0,1:T(8,128)(2,1)} %get-tuple-element.15), channel_id=1, source_target_pairs={{0,6},{2,0},{4,2},{6,4},{1,7},{3,1},{5,3},{7,5},{8,14},{10,8},{12,... | collective-permute-start | bytes 1572872 | tf_op jit(solution)/shard_map/ppermute | solution.py:74
  90.0 8.9 %copy-start.1 = (bf16[4,2,128,256]{3,2,0,1:T(8,128)(2,1)}, bf16[4,2,128,256]{3,2,0,1:T(8,128)(2,1)S(1)}, u32[]{:S(2)}) copy-start(bf16[4,2,128,256]{3,2,0,1:T(8,128)(2,1)S(1)} %collective-permute-done.6) | copy-start | bytes 1572868
  98.9 0.8 copy-start.2
  101.6 27.1 %collective-permute-start.10 = (bf16[2,128,256]{2,1,0:T(8,128)(2,1)S(1)}, bf16[2,128,256]{2,1,0:T(8,128)(2,1)S(1)}, u32[]{:S(2)}, u32[]{:S(2)}) collective-permute-start(bf16[2,128,256]{2,1,0:T(8,128)(2,1)S(1)} %get-tuple-element.20), channel_id=1, source_target_pairs={{0,16},{8,24},{16,0},{24,8},{1,17},{9,25},{17,1},{25,9},{2,18},{10... | collective-permute-start | bytes 393224 | tf_op jit(solution)/shard_map/ppermute | solution.py:74
  111.0 21.2 %collective-permute-start.11 = (bf16[2,128,256]{2,1,0:T(8,128)(2,1)S(1)}, bf16[2,128,256]{2,1,0:T(8,128)(2,1)S(1)}, u32[]{:S(2)}, u32[]{:S(2)}) collective-permute-start(bf16[2,128,256]{2,1,0:T(8,128)(2,1)S(1)} %get-tuple-element.19), channel_id=1, source_target_pairs={{0,24},{8,0},{16,8},{24,16},{1,25},{9,1},{17,9},{25,17},{2,26},{10... | collective-permute-start | bytes 393224 | tf_op jit(solution)/shard_map/ppermute | solution.py:74
  128.2 9.3 %collective-permute-start.9 = (bf16[2,128,256]{2,1,0:T(8,128)(2,1)S(1)}, bf16[2,128,256]{2,1,0:T(8,128)(2,1)S(1)}, u32[]{:S(2)}, u32[]{:S(2)}) collective-permute-start(bf16[2,128,256]{2,1,0:T(8,128)(2,1)S(1)} %get-tuple-element.18), channel_id=1, source_target_pairs={{0,8},{8,16},{16,24},{24,0},{1,9},{9,17},{17,25},{25,1},{2,10},{10... | collective-permute-start | bytes 393224 | tf_op jit(solution)/shard_map/ppermute | solution.py:74

commit v3 on v2

v3 whole, which is shorter than its diff:
```python
import functools

import jax
import jax.numpy as jnp
from jax import lax
from jax.experimental import pallas as pl
from jax.experimental.pallas import tpu as pltpu
from jax.sharding import PartitionSpec as P

REACH = 16


def _bwd_kernel(blk_ref, kb0_ref, srow_ref, dst_ref, q_ref, do_ref, kv_hbm, begin_ref,
                qpos_ref, delta_ref, dq_ref, part_ref, qall, doall, dqt, kvbuf, sems,
                *, rows, heads, width, reach, scaling):
    s = pl.program_id(0)
    win = reach + 1

    def copy(side, i):
        row = pl.multiple_of(srow_ref[side * win + i], rows)
        return pltpu.make_async_copy(
            kv_hbm.at[pl.ds(row, rows)], kvbuf.at[side, i], sems.at[side, i]
        )

    @pl.when(s == 0)
    def _():
        for side in range(2):
            for i in range(win):
                copy(side, i).start()
        part_ref[...] = jnp.zeros(part_ref.shape, jnp.float32)

    b = blk_ref[s]
    kb0 = kb0_ref[s]
    for h in range(heads):
        qall[h * rows:(h + 1) * rows, :] = q_ref[:, h * width:(h + 1) * width]
        doall[h * rows:(h + 1) * rows, :] = do_ref[:, h * width:(h + 1) * width]
    begin = begin_ref[...]
    qpos = qpos_ref[...]
    delta = delta_ref[...]
    dqt[...] = jnp.zeros(dqt.shape, jnp.float32)
    k_iota = lax.broadcasted_iota(jnp.int32, (rows, 1), 0)
    base = (b - reach) * rows
    nt = (((1,), (1,)), ((), ()))
    tn = (((0,), (0,)), ((), ()))
    for i in range(win):
        copy(s, i).wait()

    def scores(c):
        kc = kvbuf[s, c, :, :width]
        st = lax.dot_general(kc, qall[...], nt, preferred_element_type=jnp.float32) * scaling
        kpos = base + c * rows + k_iota
        allowed = (kpos >= begin) & (kpos <= qpos)
        return kc, st, allowed

    def stat_step(c, carry):
        m, l = carry
        _, st, allowed = scores(c)
        masked = jnp.where(allowed, st, -1e30)
        m_new = jnp.maximum(m, jnp.max(masked, axis=0, keepdims=True))
        e = jnp.where(allowed, jnp.exp(st - m_new), 0.0)
        l = l * jnp.exp(m - m_new) + jnp.sum(e, axis=0, keepdims=True)
        return m_new, l

    cols = heads * rows
    m0 = jnp.full((1, cols), -1e30, jnp.float32)
    l0 = jnp.zeros((1, cols), jnp.float32)
    m, l = lax.fori_loop(kb0, win, stat_step, (m0, l0))
    lse = m + jnp.log(l)

    def grad_step(c, carry):
        kc, st, allowed = scores(c)
        p = jnp.where(allowed, jnp.exp(st - lse), 0.0)
        vc = kvbuf[s, c, :, width:]
        dpt = lax.dot_general(vc, doall[...], nt, preferred_element_type=jnp.float32)
        ds = (p * (dpt - delta)).astype(jnp.bfloat16)
        pb = p.astype(jnp.bfloat16)
        dk = jnp.dot(ds, qall[...], preferred_element_type=jnp.float32) * scaling
        dv = jnp.dot(pb, doall[...], preferred_element_type=jnp.float32)
        dst = dst_ref[s * win + c]
        part_ref[dst, :, :width] += dk
        part_ref[dst, :, width:] += dv
        dqt[...] += lax.dot_general(kc, ds, tn, preferred_element_type=jnp.float32)
        return carry

    lax.fori_loop(kb0, win, grad_step, 0)
    for h in range(heads):
        piece = dqt[:, h * rows:(h + 1) * rows]
        dq_ref[:, h * width:(h + 1) * width] = (piece.T * scaling).astype(jnp.bfloat16)


def _shift(x, k, n, axis):
    return lax.ppermute(x, axis, [(i, (i + k) % n) for i in range(n)])


def _group_gather(x, n, axis):
    return jnp.stack([x] + [_shift(x, k, n, axis) for k in range(1, n)])


def _group_reduce(parts, n, axis, dim):
    me = lax.axis_index(axis)
    total = lax.dynamic_index_in_dim(parts, me, dim, keepdims=False).astype(jnp.float32)
    for k in range(1, n):
        piece = lax.dynamic_index_in_dim(parts, (me + k) % n, dim, keepdims=False)
        total = total + _shift(piece.astype(jnp.bfloat16), k, n, axis).astype(jnp.float32)
    return total


def body(queries, shared_keys, shared_values, outputs, out_grad, doc_lengths):
    n_in = lax.axis_size("w")
    rank = lax.axis_index("zp") * n_in + lax.axis_index("w")
    n_out = lax.axis_size("zp")
    n_seq = n_out * n_in
    rows = shared_keys.shape[0] // 2
    width = shared_keys.shape[1]
    heads = queries.shape[1] // width
    scaling = width ** (-0.5)
    win = REACH + 1
    doc_ends = jnp.cumsum(doc_lengths)
    doc_starts = doc_ends - doc_lengths
    blocks = jnp.stack([rank, 2 * n_seq - 1 - rank]).astype(jnp.int32)

    kv_local = jnp.concatenate([shared_keys, shared_values], axis=1)
    kv_col = _group_gather(kv_local, n_out, "zp")
    kv_recv = _group_gather(kv_col, n_in, "w").reshape(n_in * n_out * 2 * rows, 2 * width)

    me_z = lax.axis_index("zp")
    me_w = lax.axis_index("w")
    seq_blk = (blocks[:, None] - REACH + jnp.arange(win, dtype=jnp.int32)[None, :]).reshape(-1)
    seq_blk = jnp.maximum(seq_blk, 0)
    dev = jnp.where(seq_blk < n_seq, seq_blk, 2 * n_seq - 1 - seq_blk)
    slot = (seq_blk >= n_seq).astype(jnp.int32)
    k_z = (me_z - dev // n_in) % n_out
    k_w = (me_w - dev % n_in) % n_in
    srow = (((k_w * n_out + k_z) * 2 + slot) * rows).astype(jnp.int32)
    dst = (dev * 2 + slot).astype(jnp.int32)

    base_pos = jnp.arange(rows, dtype=jnp.int32)
    pos = blocks[:, None] * rows + base_pos[None, :]
    begins = jnp.max(
        jnp.where(doc_starts[None, None, :] <= pos[:, :, None], doc_starts[None, None, :], 0), axis=2
    ).astype(jnp.int32)
    kb0 = jnp.maximum(0, begins[:, 0] // rows - (blocks - REACH)).astype(jnp.int32)
    begin_t = jnp.tile(begins, (1, heads)).reshape(2, 1, heads * rows)
    qpos_t = jnp.tile(pos, (1, heads)).reshape(2, 1, heads * rows)
    prod = out_grad.astype(jnp.float32) * outputs.astype(jnp.float32)
    deltas = jnp.sum(prod.reshape(2, rows, heads, width), axis=3)
    delta_t = jnp.swapaxes(deltas, 1, 2).reshape(2, 1, heads * rows)

    kernel = functools.partial(
        _bwd_kernel, rows=rows, heads=heads, width=width, reach=REACH, scaling=scaling
    )
    cols = heads * rows
    vec = pl.BlockSpec((None, 1, cols), lambda s, *_: (s, 0, 0))
    grid_spec = pltpu.PrefetchScalarGridSpec(
        num_scalar_prefetch=4,
        grid=(2,),
        in_specs=[
            pl.BlockSpec((rows, cols), lambda s, *_: (s, 0)),
            pl.BlockSpec((rows, cols), lambda s, *_: (s, 0)),
            pl.BlockSpec(memory_space=pl.ANY),
            vec,
            vec,
            vec,
        ],
        out_specs=[
            pl.BlockSpec((rows, cols), lambda s, *_: (s, 0)),
            pl.BlockSpec((2 * n_seq, rows, 2 * width), lambda s, *_: (0, 0, 0)),
        ],
        scratch_shapes=[
            pltpu.VMEM((cols, width), jnp.bfloat16),
            pltpu.VMEM((cols, width), jnp.bfloat16),
            pltpu.VMEM((width, cols), jnp.float32),
            pltpu.VMEM((2, win, rows, 2 * width), jnp.bfloat16),
            pltpu.SemaphoreType.DMA((2, win)),
        ],
    )
    flops = 2 * 2 * win * 6 * rows * cols * width
    grad_queries, partial = pl.pallas_call(
        kernel,
        grid_spec=grid_spec,
        out_shape=[
            jax.ShapeDtypeStruct((2 * rows, cols), jnp.bfloat16),
            jax.ShapeDtypeStruct((2 * n_seq, rows, 2 * width), jnp.float32),
        ],
        compiler_params=pltpu.CompilerParams(dimension_semantics=("arbitrary",)),
        cost_estimate=pl.CostEstimate(
            flops=flops, transcendentals=2 * 2 * win * rows * cols, bytes_accessed=8 << 20
        ),
    )(blocks, kb0, srow, dst, queries, out_grad, kv_recv, begin_t, qpos_t, delta_t)

    storage = partial
    storage = storage.reshape(n_out, n_in, 2, rows, 2 * width).astype(jnp.bfloat16)
    plane = _group_reduce(storage, n_in, "w", 1)
    summed = _group_reduce(plane, n_out, "zp", 0).reshape(2 * rows, 2 * width)
    grad_keys = summed[:, :width].astype(jnp.bfloat16)
    grad_values = summed[:, width:].astype(jnp.bfloat16)
    return (grad_queries, grad_keys, grad_values)


GROUP = 4


def solution(mesh):
    n_seq, n_grp = mesh.devices.shape
    split = mesh.devices.reshape(n_seq // GROUP, GROUP, n_grp)
    mesh2 = jax.sharding.Mesh(split, ("zp", "w", "grp"))
    rows = P(("zp", "w"), "grp")
    placed = (rows, rows, rows, rows, rows, P())
    return jax.shard_map(
        body,
        mesh=mesh2,
        in_specs=placed,
        out_specs=(rows, rows, rows),
        check_vma=False,
    )
```

time: 140 us -> 118 us (0.84); the launches traced: 138 us -> 119 us
  local copies, waits for them, and re-layouts: 18.3 us -> 5.78 us
  starting transfers between devices: 44.4 us -> 36.9 us
  other arithmetic: 12.5 us -> 9.11 us
  Pallas kernels: 7.74 us -> 10.5 us
  waiting for transfers between devices: 54.5 us -> 56.1 us
    ppermute x12, starting transfers between devices: 44.4 us -> 36.9 us  [_shift(): return lax.ppermute(x, axis, [(i, (i + k) % n) for i in range(n)])]
    another operation x2 -> x1, local copies, waits for them, and re-layouts: 4.26 us -> 0.1 us  [the longest x1 4.16 us: body(): jnp.stack([lax.dynamic_slice_in_dim(kv_seq, blocks[i], win, 0) for i in r...]
    unnamed x14 -> x6, local copies, waits for them, and re-layouts: 4.26 us -> 1.11 us
    pallas_call x1, Pallas kernels: 7.74 us -> 10.5 us  [body(): pl.pallas_call(kernel, grid_spec=grid_spec, out_shape=[jax.ShapeDtypeStru...]
    gather x2 -> x0, local copies, waits for them, and re-layouts: 2.59 us -> none  [_group_gather(): return jnp.take(got, order, axis=0)]
    convert_element_type x0 -> x1, other arithmetic: none -> 2.47 us  [body(): storage.reshape(n_out, n_in, 2, rows, 2 * width).astype(jnp.bfloat16)]
    select_n x5 -> x0, other arithmetic: 2.11 us -> none  [_group_gather(): return jnp.take(got, order, axis=0)]
    dynamic_slice x3 -> x0, local copies, waits for them, and re-layouts: 1.83 us -> none  [body(): lax.dynamic_slice_in_dim(kv_seq, blocks[i], win, 0)]
  transfers between devices with their start and end apart: 12 -> 12, of which waited for: 9 -> 9; matrix products, arithmetic and copies ran while one was open for 3% -> 4% of each run, Pallas kernels for 0% -> 0%
where the time goes in v3:
time: 118 us; the launch traced here: 119 us
  waiting for transfers between devices  56.1 us (48%)
  starting transfers between devices  36.9 us (31%)
  Pallas kernels  10.5 us (9%)
  other arithmetic  9.11 us (8%)
  local copies, waits for them, and re-layouts  5.78 us (5%)
    ppermute x12, waiting for transfers between devices, _shift(): return lax.ppermute(x, axis, [(i, (i + k) % n) for i in range(n)])  56.1 us
    ppermute x12, starting transfers between devices, _shift(): return lax.ppermute(x, axis, [(i, (i + k) % n) for i in range(n)])  36.9 us
    pallas_call x1, Pallas kernels, body(): pl.pallas_call(kernel, grid_spec=grid_spec, out_shape=[jax.ShapeDtypeStru...  10.5 us
    convert_element_type x1, other arithmetic, body(): storage.reshape(n_out, n_in, 2, rows, 2 * width).astype(jnp.bfloat16)  2.47 us
  transfers between devices with their start and end apart: 12, of which 9 were waited for; matrix products, arithmetic and copies ran while one was open for 4% of the time, Pallas kernels for 0%

profile of v3, /device:TPU:0, one launch (start us, length us, event | category | flops | bytes accessed | tf_op | source)
XLA Modules:
  0.0 119.2 jit_solution(12270814783490818370)
XLA Ops:
  0.6 0.9 constant_dynamic-update-slice_fusion.1
  1.5 0.9 constant_dynamic-update-slice_fusion
  2.3 3.1 %collective-permute-start = (bf16[256,256]{1,0:T(8,128)(2,1)S(1)}, bf16[256,256]{1,0:T(8,128)(2,1)S(1)}, u32[]{:S(2)}, u32[]{:S(2)}) collective-permute-start(bf16[256,256]{1,0:T(8,128)(2,1)S(1)} %constant_dynamic-update-slice_fusion), channel_id=1, source_target_pairs={{0,8},{8,16},{16,24},{24,0},{1,9},{9,17},{17,25},{25,1},{2,10},{10... | collective-permute-start | bytes 393224 | tf_op jit(solution)/shard_map/ppermute | solution.py:92
  5.5 2.6 %collective-permute-start.1 = (bf16[256,256]{1,0:T(8,128)(2,1)S(1)}, bf16[256,256]{1,0:T(8,128)(2,1)S(1)}, u32[]{:S(2)}, u32[]{:S(2)}) collective-permute-start(bf16[256,256]{1,0:T(8,128)(2,1)S(1)} %constant_dynamic-update-slice_fusion), channel_id=1, source_target_pairs={{0,16},{8,24},{16,0},{24,8},{1,17},{9,25},{17,1},{25,9},{2,18},{10... | collective-permute-start | bytes 393224 | tf_op jit(solution)/shard_map/ppermute | solution.py:92
  8.0 1.3 %collective-permute-start.2 = (bf16[256,256]{1,0:T(8,128)(2,1)S(1)}, bf16[256,256]{1,0:T(8,128)(2,1)S(1)}, u32[]{:S(2)}, u32[]{:S(2)}) collective-permute-start(bf16[256,256]{1,0:T(8,128)(2,1)S(1)} %constant_dynamic-update-slice_fusion), channel_id=1, source_target_pairs={{0,24},{8,0},{16,8},{24,16},{1,25},{9,1},{17,9},{25,17},{2,26},{10... | collective-permute-start | bytes 393224 | tf_op jit(solution)/shard_map/ppermute | solution.py:92
  9.4 0.1 broadcast_add_fusion
  9.5 0.1 iota_add_fusion
  9.5 0.1 add_maximum_fusion
  9.6 1.4 %multiply_bitcast_fusion = f32[32,8,8,128]{3,1,2,0:T(8,128)S(1)} fusion(bf16[256,1024]{1,0:T(8,128)(2,1)} %param.9, bf16[256,1024]{1,0:T(8,128)(2,1)} %do_ref.1), kind=kLoop, calls=%fused_computation.5 | loop fusion | flops 786432 | bytes 2097152
  11.0 0.0 copy-start
  11.0 0.2 copy.20
  11.2 0.3 bitcast_reduce_fusion
  11.6 0.1 copy-done
  11.7 0.1 copy.18
  11.8 0.1 reduce-window.9
  11.8 0.1 reduce
  12.0 0.1 max.17
  12.1 0.7 copy.19
  12.7 0.1 select_reduce_fusion
  12.8 3.9 %collective-permute-done.1 = bf16[256,256]{1,0:T(8,128)(2,1)S(1)} collective-permute-done((bf16[256,256]{1,0:T(8,128)(2,1)S(1)}, bf16[256,256]{1,0:T(8,128)(2,1)S(1)}, u32[]{:S(2)}, u32[]{:S(2)}) %collective-permute-start.1) | collective-permute-done | bytes 131104 | tf_op jit(solution)/shard_map/ppermute | solution.py:92
  16.7 0.1 fusion.13
  16.8 2.5 %collective-permute-start.5 = (bf16[4,256,256]{2,1,0:T(8,128)(2,1)S(1)}, bf16[4,256,256]{2,1,0:T(8,128)(2,1)S(1)}, u32[]{:S(2)}, u32[]{:S(2)}) collective-permute-start(bf16[4,256,256]{2,1,0:T(8,128)(2,1)S(1)} %get-tuple-element.16), channel_id=1, source_target_pairs={{0,6},{2,0},{4,2},{6,4},{1,7},{3,1},{5,3},{7,5},{8,14},{10,8},{12,... | collective-permute-start | bytes 1572872 | tf_op jit(solution)/shard_map/ppermute | solution.py:92
  19.3 1.1 collective-permute-start.4
  20.4 0.1 slice_reduce_fusion
  20.5 0.5 subtract_maximum_fusion.kb0_ref
  21.0 0.5 multiply_add_fusion
  21.6 10.1 %collective-permute-done.5 = bf16[4,256,256]{2,1,0:T(8,128)(2,1)S(1)} collective-permute-done((bf16[4,256,256]{2,1,0:T(8,128)(2,1)S(1)}, bf16[4,256,256]{2,1,0:T(8,128)(2,1)S(1)}, u32[]{:S(2)}, u32[]{:S(2)}) %collective-permute-start.5) | collective-permute-done | bytes 524320 | tf_op jit(solution)/shard_map/ppermute | solution.py:92
  31.6 11.2 %collective-permute-done.3 = bf16[4,256,256]{2,1,0:T(8,128)(2,1)S(1)} collective-permute-done((bf16[4,256,256]{2,1,0:T(8,128)(2,1)S(1)}, bf16[4,256,256]{2,1,0:T(8,128)(2,1)S(1)}, u32[]{:S(2)}, u32[]{:S(2)}) %collective-permute-start.3) | collective-permute-done | bytes 524320 | tf_op jit(solution)/shard_map/ppermute | solution.py:92
  42.9 1.1 collective-permute-done.4
  44.0 1.6 %pad_maximum_fusion = bf16[4,4,256,256]{3,2,1,0:T(8,128)(2,1)} fusion(bf16[1,4,256,256]{3,2,1,0:T(8,128)(2,1)S(1)} %bitcast.54, bf16[1,4,256,256]{3,2,1,0:T(8,128)(2,1)S(1)} %bitcast.56, bf16[1,4,256,256]{3,2,1,0:T(8,128)(2,1)S(1)} %bitcast.55, bf16[1,4,256,256]{3,2,1,0:T(8,128)(2,1)S(1)} %get-tuple-element.15), kind=kLoop, calls=%fused_computation | loop fusion | flops 3145728 | bytes 4194304 | tf_op jit(solution)/shard_map/stack | solution.py:96
  45.6 0.6 tile.16
  46.2 0.6 tile.18
  46.8 10.5 %shard_map.85 = (bf16[256,1024]{1,0:T(8,128)(2,1)}, f32[32,128,256]{2,1,0:T(8,128)}) custom-call(s32[2]{0:T(128)} %copy-done.1, s32[2]{0:T(128)} %subtract_maximum_fusion.kb0_ref, s32[34]{0:T(128)} %get-tuple-element.20.srow_ref, s32[34]{0:T(128)} %get-tuple-element.19.dst_ref, bf16[256,1024]{1,0:T(8,128)(2,1)} %q_ref.1, bf16[256,1024]{1,0:T(8,128)(2,1)} %do_ref.1, ...), custom_call_target="tpu_custom_call" | custom-call | flops 6845104128 | bytes 8388608 | tf_op jit(solution)/shard_map/pallas_call | solution.py:178
  57.3 2.5 %convert_element_type.62 = bf16[32,128,256]{2,1,0:T(8,128)(2,1)S(1)} convert(f32[32,128,256]{2,1,0:T(8,128)} %get-tuple-element.6) | non-fusion elementwise | flops 1048576 | bytes 6291456 | tf_op jit(solution)/shard_map/convert_element_type | solution.py:192
  59.8 0.9 dynamic-slice_bitcast_fusion.2
  60.7 2.3 %collective-permute-start.6 = (bf16[4,2,128,256]{3,2,1,0:T(8,128)(2,1)}, bf16[4,2,128,256]{3,2,1,0:T(8,128)(2,1)}, u32[]{:S(2)}, u32[]{:S(2)}) collective-permute-start(bf16[4,2,128,256]{3,2,1,0:T(8,128)(2,1)} %get-tuple-element.9), channel_id=1, source_target_pairs={{0,2},{2,4},{4,6},{6,0},{1,3},{3,5},{5,7},{7,1},{8,10},{10,12},{12... | collective-permute-start | bytes 1572872 | tf_op jit(solution)/shard_map/ppermute | solution.py:92
  63.1 2.8 %collective-permute-start.8 = (bf16[4,2,128,256]{3,2,1,0:T(8,128)(2,1)S(1)}, bf16[4,2,128,256]{3,2,1,0:T(8,128)(2,1)}, u32[]{:S(2)}, u32[]{:S(2)}) collective-permute-start(bf16[4,2,128,256]{3,2,1,0:T(8,128)(2,1)S(1)} %get-tuple-element.10), channel_id=1, source_target_pairs={{0,6},{2,0},{4,2},{6,4},{1,7},{3,1},{5,3},{7,5},{8,14},{10,8},{12,... | collective-permute-start | bytes 1572872 | tf_op jit(solution)/shard_map/ppermute | solution.py:92
  65.9 10.9 %collective-permute-done.6 = bf16[4,2,128,256]{3,2,1,0:T(8,128)(2,1)} collective-permute-done((bf16[4,2,128,256]{3,2,1,0:T(8,128)(2,1)}, bf16[4,2,128,256]{3,2,1,0:T(8,128)(2,1)}, u32[]{:S(2)}, u32[]{:S(2)}) %collective-permute-start.6) | collective-permute-done | bytes 524320 | tf_op jit(solution)/shard_map/ppermute | solution.py:92
  76.8 9.1 %collective-permute-done.7 = bf16[4,2,128,256]{3,2,1,0:T(8,128)(2,1)} collective-permute-done((bf16[4,2,128,256]{3,2,1,0:T(8,128)(2,1)S(1)}, bf16[4,2,128,256]{3,2,1,0:T(8,128)(2,1)}, u32[]{:S(2)}, u32[]{:S(2)}) %collective-permute-start.7) | collective-permute-done | bytes 524320 | tf_op jit(solution)/shard_map/ppermute | solution.py:92
  85.8 0.8 collective-permute-done.8
  86.7 1.6 %fusion.1 = f32[4,2,128,256]{3,2,1,0:T(8,128)S(1)} fusion(bf16[4,2,128,256]{3,2,1,0:T(8,128)(2,1)} %collective-permute-done.8, bf16[4,2,128,256]{3,2,1,0:T(8,128)(2,1)} %collective-permute-done.7, bf16[4,2,128,256]{3,2,1,0:T(8,128)(2,1)} %collective-permute-done.6, bf16[4,4,2,128,256]{4,3,2,1,0:T(8,128)(2,1)S(1)} %bitcast.49, s32[]{:T(128)S(6)} %select_n.91), kind=kLoop, calls=%fused_computation.4 | loop fusion | flops 1835008 | bytes 3145732 | tf_op jit(solution)/shard_map/add | solution.py:104
  88.3 0.1 fusion.5
  88.3 15.5 %collective-permute-start.10 = (bf16[2,128,256]{2,1,0:T(8,128)(2,1)S(1)}, bf16[2,128,256]{2,1,0:T(8,128)(2,1)S(1)}, u32[]{:S(2)}, u32[]{:S(2)}) collective-permute-start(bf16[2,128,256]{2,1,0:T(8,128)(2,1)S(1)} %get-tuple-element.14), channel_id=1, source_target_pairs={{0,16},{8,24},{16,0},{24,8},{1,17},{9,25},{17,1},{25,9},{2,18},{10... | collective-permute-start | bytes 393224 | tf_op jit(solution)/shard_map/ppermute | solution.py:92
  103.8 5.6 %collective-permute-start.11 = (bf16[2,128,256]{2,1,0:T(8,128)(2,1)S(1)}, bf16[2,128,256]{2,1,0:T(8,128)(2,1)S(1)}, u32[]{:S(2)}, u32[]{:S(2)}) collective-permute-start(bf16[2,128,256]{2,1,0:T(8,128)(2,1)S(1)} %get-tuple-element.13), channel_id=1, source_target_pairs={{0,24},{8,0},{16,8},{24,16},{1,25},{9,1},{17,9},{25,17},{2,26},{10... | collective-permute-start | bytes 393224 | tf_op jit(solution)/shard_map/ppermute | solution.py:92
  109.5 3.9 %collective-permute-done.11 = bf16[2,128,256]{2,1,0:T(8,128)(2,1)S(1)} collective-permute-done((bf16[2,128,256]{2,1,0:T(8,128)(2,1)S(1)}, bf16[2,128,256]{2,1,0:T(8,128)(2,1)S(1)}, u32[]{:S(2)}, u32[]{:S(2)}) %collective-permute-start.11) | collective-permute-done | bytes 131104 | tf_op jit(solution)/shard_map/ppermute | solution.py:92
  113.3 5.2 %collective-permute-done.9 = bf16[2,128,256]{2,1,0:T(8,128)(2,1)S(1)} collective-permute-done((bf16[2,128,256]{2,1,0:T(8,128)(2,1)S(1)}, bf16[2,128,256]{2,1,0:T(8,128)(2,1)S(1)}, u32[]{:S(2)}, u32[]{:S(2)}) %collective-permute-start.9) | collective-permute-done | bytes 131104 | tf_op jit(solution)/shard_map/ppermute | solution.py:92
  118.5 0.1 fusion.4
  118.6 0.7 fusion.14
  (10 shorter events, 0.0 us)
Async XLA Ops:
  2.3 10.5 %collective-permute-start = (bf16[256,256]{1,0:T(8,128)(2,1)S(1)}, bf16[256,256]{1,0:T(8,128)(2,1)S(1)}, u32[]{:S(2)}, u32[]{:S(2)}) collective-permute-start(bf16[256,256]{1,0:T(8,128)(2,1)S(1)} %constant_dynamic-update-slice_fusion), channel_id=1, source_target_pairs={{0,8},{8,16},{16,24},{24,0},{1,9},{9,17},{17,25},{25,1},{2,10},{10... | collective-permute-start | bytes 393224 | tf_op jit(solution)/shard_map/ppermute | solution.py:92
  5.5 11.2 %collective-permute-start.1 = (bf16[256,256]{1,0:T(8,128)(2,1)S(1)}, bf16[256,256]{1,0:T(8,128)(2,1)S(1)}, u32[]{:S(2)}, u32[]{:S(2)}) collective-permute-start(bf16[256,256]{1,0:T(8,128)(2,1)S(1)} %constant_dynamic-update-slice_fusion), channel_id=1, source_target_pairs={{0,16},{8,24},{16,0},{24,8},{1,17},{9,25},{17,1},{25,9},{2,18},{10... | collective-permute-start | bytes 393224 | tf_op jit(solution)/shard_map/ppermute | solution.py:92
  8.0 8.6 %collective-permute-start.2 = (bf16[256,256]{1,0:T(8,128)(2,1)S(1)}, bf16[256,256]{1,0:T(8,128)(2,1)S(1)}, u32[]{:S(2)}, u32[]{:S(2)}) collective-permute-start(bf16[256,256]{1,0:T(8,128)(2,1)S(1)} %constant_dynamic-update-slice_fusion), channel_id=1, source_target_pairs={{0,24},{8,0},{16,8},{24,16},{1,25},{9,1},{17,9},{25,17},{2,26},{10... | collective-permute-start | bytes 393224 | tf_op jit(solution)/shard_map/ppermute | solution.py:92
  9.5 11.0 %copy-start.1 = (s32[2]{0:T(128)}, s32[2]{0:T(128)S(1)}, u32[]{:S(2)}) copy-start(s32[2]{0:T(128)S(1)} %get-tuple-element.8.blk_ref) | copy-start | bytes 28
  11.0 0.7 copy-start
  16.8 14.9 %collective-permute-start.5 = (bf16[4,256,256]{2,1,0:T(8,128)(2,1)S(1)}, bf16[4,256,256]{2,1,0:T(8,128)(2,1)S(1)}, u32[]{:S(2)}, u32[]{:S(2)}) collective-permute-start(bf16[4,256,256]{2,1,0:T(8,128)(2,1)S(1)} %get-tuple-element.16), channel_id=1, source_target_pairs={{0,6},{2,0},{4,2},{6,4},{1,7},{3,1},{5,3},{7,5},{8,14},{10,8},{12,... | collective-permute-start | bytes 1572872 | tf_op jit(solution)/shard_map/ppermute | solution.py:92
  19.3 23.6 %collective-permute-start.3 = (bf16[4,256,256]{2,1,0:T(8,128)(2,1)S(1)}, bf16[4,256,256]{2,1,0:T(8,128)(2,1)S(1)}, u32[]{:S(2)}, u32[]{:S(2)}) collective-permute-start(bf16[4,256,256]{2,1,0:T(8,128)(2,1)S(1)} %get-tuple-element.16), channel_id=1, source_target_pairs={{0,2},{2,4},{4,6},{6,0},{1,3},{3,5},{5,7},{7,1},{8,10},{10,12},{12... | collective-permute-start | bytes 1572872 | tf_op jit(solution)/shard_map/ppermute | solution.py:92
  19.3 24.7 %collective-permute-start.4 = (bf16[4,256,256]{2,1,0:T(8,128)(2,1)S(1)}, bf16[4,256,256]{2,1,0:T(8,128)(2,1)S(1)}, u32[]{:S(2)}, u32[]{:S(2)}) collective-permute-start(bf16[4,256,256]{2,1,0:T(8,128)(2,1)S(1)} %get-tuple-element.16), channel_id=1, source_target_pairs={{0,4},{2,6},{4,0},{6,2},{1,5},{3,7},{5,1},{7,3},{8,12},{10,14},{12... | collective-permute-start | bytes 1572872 | tf_op jit(solution)/shard_map/ppermute | solution.py:92
  60.7 16.1 %collective-permute-start.6 = (bf16[4,2,128,256]{3,2,1,0:T(8,128)(2,1)}, bf16[4,2,128,256]{3,2,1,0:T(8,128)(2,1)}, u32[]{:S(2)}, u32[]{:S(2)}) collective-permute-start(bf16[4,2,128,256]{3,2,1,0:T(8,128)(2,1)} %get-tuple-element.9), channel_id=1, source_target_pairs={{0,2},{2,4},{4,6},{6,0},{1,3},{3,5},{5,7},{7,1},{8,10},{10,12},{12... | collective-permute-start | bytes 1572872 | tf_op jit(solution)/shard_map/ppermute | solution.py:92
  63.1 22.8 %collective-permute-start.7 = (bf16[4,2,128,256]{3,2,1,0:T(8,128)(2,1)S(1)}, bf16[4,2,128,256]{3,2,1,0:T(8,128)(2,1)}, u32[]{:S(2)}, u32[]{:S(2)}) collective-permute-start(bf16[4,2,128,256]{3,2,1,0:T(8,128)(2,1)S(1)} %get-tuple-element.11), channel_id=1, source_target_pairs={{0,4},{2,6},{4,0},{6,2},{1,5},{3,7},{5,1},{7,3},{8,12},{10,14},{12... | collective-permute-start | bytes 1572872 | tf_op jit(solution)/shard_map/ppermute | solution.py:92
  63.1 23.6 %collective-permute-start.8 = (bf16[4,2,128,256]{3,2,1,0:T(8,128)(2,1)S(1)}, bf16[4,2,128,256]{3,2,1,0:T(8,128)(2,1)}, u32[]{:S(2)}, u32[]{:S(2)}) collective-permute-start(bf16[4,2,128,256]{3,2,1,0:T(8,128)(2,1)S(1)} %get-tuple-element.10), channel_id=1, source_target_pairs={{0,6},{2,0},{4,2},{6,4},{1,7},{3,1},{5,3},{7,5},{8,14},{10,8},{12,... | collective-permute-start | bytes 1572872 | tf_op jit(solution)/shard_map/ppermute | solution.py:92
  88.3 21.1 %collective-permute-start.10 = (bf16[2,128,256]{2,1,0:T(8,128)(2,1)S(1)}, bf16[2,128,256]{2,1,0:T(8,128)(2,1)S(1)}, u32[]{:S(2)}, u32[]{:S(2)}) collective-permute-start(bf16[2,128,256]{2,1,0:T(8,128)(2,1)S(1)} %get-tuple-element.14), channel_id=1, source_target_pairs={{0,16},{8,24},{16,0},{24,8},{1,17},{9,25},{17,1},{25,9},{2,18},{10... | collective-permute-start | bytes 393224 | tf_op jit(solution)/shard_map/ppermute | solution.py:92
  103.8 9.5 %collective-permute-start.11 = (bf16[2,128,256]{2,1,0:T(8,128)(2,1)S(1)}, bf16[2,128,256]{2,1,0:T(8,128)(2,1)S(1)}, u32[]{:S(2)}, u32[]{:S(2)}) collective-permute-start(bf16[2,128,256]{2,1,0:T(8,128)(2,1)S(1)} %get-tuple-element.13), channel_id=1, source_target_pairs={{0,24},{8,0},{16,8},{24,16},{1,25},{9,1},{17,9},{25,17},{2,26},{10... | collective-permute-start | bytes 393224 | tf_op jit(solution)/shard_map/ppermute | solution.py:92
  109.4 9.1 %collective-permute-start.9 = (bf16[2,128,256]{2,1,0:T(8,128)(2,1)S(1)}, bf16[2,128,256]{2,1,0:T(8,128)(2,1)S(1)}, u32[]{:S(2)}, u32[]{:S(2)}) collective-permute-start(bf16[2,128,256]{2,1,0:T(8,128)(2,1)S(1)} %get-tuple-element.12), channel_id=1, source_target_pairs={{0,8},{8,16},{16,24},{24,0},{1,9},{9,17},{17,25},{25,1},{2,10},{10... | collective-permute-start | bytes 393224 | tf_op jit(solution)/shard_map/ppermute | solution.py:92
